TPU v7x, 128 devices: a whole 4x4x4 slice. The times are simulated.
128 devices in a mesh: grp: 8 (over z, core), dev: 16 (over y, x).
Axes of the slice: x: 4, y: 4, z: 4, core: 2. Of those that a mesh axis runs over, the one named last changes fastest.
Arguments:
- positions: float32 [3, 131072], P(None, ('grp', 'dev')), may hold values from -3 to 3
- velocities: float32 [3, 131072], P(None, ('grp', 'dev')), may hold values from -5 to 5
- accelerations: float32 [3, 131072], P(None, ('grp', 'dev')), may hold values from -3 to 3
- jerks: float32 [3, 131072], P(None, ('grp', 'dev')), may hold values from -3 to 3
- levels: int32 [131072], P(('grp', 'dev')), may hold values from 0 to 5
- counts: int32 [2, 128], replicated, may hold values from 1 to 256, 16384 in all within a row
- active_rows: int32 [2, 32768], P(None, ('grp', 'dev')), may hold values from 0 to 1023, as said below
Outputs:
- new_positions: float32 [3, 131072], P(None, ('grp', 'dev'))
- new_velocities: float32 [3, 131072], P(None, ('grp', 'dev'))
- new_accelerations: float32 [3, 131072], P(None, ('grp', 'dev'))
- new_jerks: float32 [3, 131072], P(None, ('grp', 'dev'))
Inputs may be any that keep to these rules, and one draw needn't show every extreme that they name: In each step the 128 counts sum to exactly 16384 and the largest of them is exactly 256. `active_rows`: for each step and device, the 256 entries of the device's slots are distinct indices of that device's own stars; only the first counts of them are live.
All inputs are finite; a program needn't handle non-finite values.
Results may differ from a plain program's by a relative error of at most 0.00022.
Values sent between devices are 32-bit elements; how exact they have to be, the bound alone decides.
No kernel may reach another device: no remote copies, remote signals or barrier semaphores. Data moves between devices by JAX's collectives and lax.ppermute only.
A program may use at most 128 MiB of HBM per device.

v0:
```python
import math
import jax
import jax.numpy as jnp
from jax import lax
from jax.sharding import PartitionSpec as P

tick_length = 1.0 / 128.0


def pair_block(targets, src_pos, src_vel, mass, soft_sq):
    gap_x = src_pos[0][None, :] - targets[0][:, None]
    gap_y = src_pos[1][None, :] - targets[1][:, None]
    gap_z = src_pos[2][None, :] - targets[2][:, None]
    drift_x = src_vel[0][None, :] - targets[3][:, None]
    drift_y = src_vel[1][None, :] - targets[4][:, None]
    drift_z = src_vel[2][None, :] - targets[5][:, None]
    squared = gap_x * gap_x + gap_y * gap_y + gap_z * gap_z + soft_sq
    inverse = lax.rsqrt(squared)
    weight = mass * inverse * inverse * inverse
    along = 3.0 * (gap_x * drift_x + gap_y * drift_y + gap_z * drift_z) * inverse * inverse
    return jnp.stack(
        [
            jnp.sum(weight * gap_x, axis=1),
            jnp.sum(weight * gap_y, axis=1),
            jnp.sum(weight * gap_z, axis=1),
            jnp.sum(weight * (drift_x - along * gap_x), axis=1),
            jnp.sum(weight * (drift_y - along * gap_y), axis=1),
            jnp.sum(weight * (drift_z - along * gap_z), axis=1),
        ]
    )


def block_terms(packed, src_pos, src_vel, mass, soft_sq):
    width, total = packed.shape
    block = math.gcd(total, 2048)
    grouped = packed.reshape(width, total // block, block).transpose(1, 0, 2)
    result = lax.map(lambda targets: pair_block(targets, src_pos, src_vel, mass, soft_sq), grouped)
    return result.transpose(1, 0, 2).reshape(width, total)


def predict(positions, velocities, accelerations, jerks, elapsed):
    span = elapsed[None, :]
    pred_pos = (
        positions
        + span * velocities
        + 0.5 * span * span * accelerations
        + span * span * span / 6.0 * jerks
    )
    pred_vel = velocities + span * accelerations + 0.5 * span * span * jerks
    return (pred_pos, pred_vel)


def correct(old_pos, old_vel, old_acc, old_jerk, force, jerk_new, span):
    span = span[None, :]
    new_vel = old_vel + 0.5 * span * (old_acc + force) + span * span / 12.0 * (old_jerk - jerk_new)
    new_pos = old_pos + 0.5 * span * (old_vel + new_vel) + span * span / 12.0 * (old_acc - force)
    return (new_pos, new_vel)


def shards(positions, velocities, accelerations, jerks, levels, counts, active_rows):
    devices_all = lax.axis_size("grp") * lax.axis_size("dev")
    my_rank = lax.axis_index("grp") * lax.axis_size("dev") + lax.axis_index("dev")
    star_dev = positions.shape[1]
    slot_cap = active_rows.shape[1]
    stars_all = star_dev * devices_all
    live_all = stars_all // 8
    mass = 1.0 / stars_all
    soft_sq = 0.0004 * (131072.0 / stars_all) ** (2.0 / 3.0)
    chunks = 4
    chunk = live_all // chunks
    last_time = -(jnp.left_shift(jnp.int32(1), levels) - 1).astype(jnp.float32) * tick_length
    for step in range(active_rows.shape[0]):
        now = (step + 1) * tick_length
        pred_pos, pred_vel = predict(positions, velocities, accelerations, jerks, now - last_time)
        rows = active_rows[step]
        targets = jnp.concatenate([pred_pos[:, rows], pred_vel[:, rows]], axis=0)
        step_counts = counts[step]
        own_count = step_counts[my_rank]
        inclusive = jnp.cumsum(step_counts).astype(jnp.int32)
        first = inclusive - step_counts
        place = jnp.arange(live_all, dtype=jnp.int32)
        owner = jnp.sum((inclusive[None, :] <= place[:, None]).astype(jnp.int32), axis=1)
        owner = jnp.minimum(owner, devices_all - 1)
        slot = owner * slot_cap + place - first[owner]
        gathered = lax.all_gather(targets[None], ("grp", "dev"), axis=0, tiled=True)
        flat = gathered.transpose(1, 0, 2).reshape(6, devices_all * slot_cap)
        compact = flat[:, slot]
        parts = []
        summed = None
        for c in range(chunks):
            piece = compact[:, c * chunk : (c + 1) * chunk]
            terms = block_terms(piece, pred_pos, pred_vel, mass, soft_sq)
            if summed is not None:
                terms, summed = lax.optimization_barrier((terms, summed))
                parts.append(summed)
            summed = lax.psum(terms, ("grp", "dev"))
        parts.append(summed)
        parts.append(jnp.zeros((6, slot_cap), jnp.float32))
        totals = jnp.concatenate(parts, axis=1)
        own = lax.dynamic_slice_in_dim(totals, first[my_rank], slot_cap, 1)
        span = now - last_time[rows]
        new_pos, new_vel = correct(
            positions[:, rows],
            velocities[:, rows],
            accelerations[:, rows],
            jerks[:, rows],
            own[:3],
            own[3:],
            span,
        )
        live = jnp.arange(slot_cap, dtype=jnp.int32) < own_count
        target = jnp.where(live, rows, star_dev)
        positions = positions.at[:, target].set(new_pos, mode="drop")
        velocities = velocities.at[:, target].set(new_vel, mode="drop")
        accelerations = accelerations.at[:, target].set(own[:3], mode="drop")
        jerks = jerks.at[:, target].set(own[3:], mode="drop")
        last_time = last_time.at[target].set(now, mode="drop")
    return (positions, velocities, accelerations, jerks)


def solution(mesh):
    placed = (
        P(None, ("grp", "dev")),
        P(None, ("grp", "dev")),
        P(None, ("grp", "dev")),
        P(None, ("grp", "dev")),
        P(("grp", "dev")),
        P(),
        P(None, ("grp", "dev")),
    )
    return jax.shard_map(
        shards,
        mesh=mesh,
        in_specs=placed,
        out_specs=(
            P(None, ("grp", "dev")),
            P(None, ("grp", "dev")),
            P(None, ("grp", "dev")),
            P(None, ("grp", "dev")),
        ),
        check_vma=False,
    )
```

profile of v0, /device:TPU:1, one launch (start us, length us, event | category | flops | bytes accessed | tf_op | source)
XLA Modules:
  0.0 1731.8 jit_solution(9103468403013295511)
XLA Ops:
  14.8 63.9 %all-gather.2 = f32[128,6,256]{2,1,0:T(8,128)S(1)} all-gather(f32[1,6,256]{2,1,0:T(8,128)S(1)} %maximum_bitcast_fusion), channel_id=2, replica_groups=mesh['grp'=8,'dev'=16] {'grp','dev'}, dimensions={0}, use_global_device_ids=true | all-gather | bytes 792576 | tf_op jit(solution)/shard_map/all_gather | solution.py:85
  90.3 97.2 %gather_fusion.6 = s32[16384]{0:T(1024)S(1)} fusion(s32[128]{0:T(128)S(1)} %get-tuple-element.734, s32[16384]{0:T(1024)S(1)} %broadcast_clamp_fusion.3), kind=kCustom, calls=%fused_computation.6 | custom fusion | bytes 196608 | tf_op jit(solution)/shard_map/gather | solution.py:84
  187.7 60.2 %gather_fusion.7 = f32[16384,6]{1,0:T(8,128)} fusion(f32[6,32768]{0,1:T(8,128)} %bitcast.632, s32[16384]{0:T(1024)S(1)} %broadcast_clamp_fusion.1), kind=kCustom, calls=%fused_computation.7 | custom fusion | bytes 851968 | tf_op jit(solution)/shard_map/gather | solution.py:87
  256.3 32.8 %while.81 = (s32[]{:T(128)}, f32[2,6,2048]{2,1,0:T(8,128)S(1)}, f32[3,1024]{1,0:T(4,128)S(1)}, f32[2,6,2048]{2,1,0:T(8,128)S(1)}, f32[3,1024]{1,0:T(4,128)S(1)},...) while((s32[]{:T(128)}, f32[2,6,2048]{2,1,0:T(8,128)S(1)}, ...), condition=%wide.region_17.18_spmd, body=%wide.region_10.17_spmd.sunk | while | flops 85970952 | bytes 499925 | solution.py:37
  272.8 16.2 fusion.187
  294.7 32.8 %while.80 = (s32[]{:T(128)}, f32[2,6,2048]{2,1,0:T(8,128)S(1)}, f32[3,1024]{1,0:T(4,128)S(1)}, f32[2,6,2048]{2,1,0:T(8,128)S(1)}, f32[3,1024]{1,0:T(4,128)S(1)},...) while((s32[]{:T(128)}, f32[2,6,2048]{2,1,0:T(8,128)S(1)}, ...), condition=%wide.region_9.10_spmd, body=%wide.region_2.9_spmd.sunk | while | flops 85970952 | bytes 499925 | solution.py:37
  329.8 32.8 %while.82 = (s32[]{:T(128)}, f32[2,6,2048]{2,1,0:T(8,128)S(1)}, f32[3,1024]{1,0:T(4,128)S(1)}, f32[2,6,2048]{2,1,0:T(8,128)S(1)}, f32[3,1024]{1,0:T(4,128)S(1)},...) while((s32[]{:T(128)}, f32[2,6,2048]{2,1,0:T(8,128)S(1)}, ...), condition=%wide.region_26.27_spmd, body=%wide.region_19.26_spmd.sunk | while | flops 85970952 | bytes 499925 | solution.py:37
  363.3 32.9 %while.83 = (s32[]{:T(128)}, f32[2,6,2048]{2,1,0:T(8,128)S(1)}, f32[3,1024]{1,0:T(4,128)S(1)}, f32[2,6,2048]{2,1,0:T(8,128)S(1)}, f32[3,1024]{1,0:T(4,128)S(1)},...) while((s32[]{:T(128)}, f32[2,6,2048]{2,1,0:T(8,128)S(1)}, ...), condition=%wide.region_35.36_spmd, body=%wide.region_28.35_spmd.sunk | while | flops 85970952 | bytes 499925 | solution.py:37
  363.4 16.2 fusion.191
  379.9 16.2 fusion.191
  399.8 97.2 %gather_fusion.15 = s32[16384]{0:T(1024)S(1)} fusion(s32[128]{0:T(128)S(1)} %get-tuple-element.733, s32[16384]{0:T(1024)S(1)} %broadcast_clamp_fusion.2), kind=kCustom, calls=%fused_computation.15 | custom fusion | bytes 196608 | tf_op jit(solution)/shard_map/gather | solution.py:84
  509.3 137.8 %all-reduce.11.cloned.1.call-done = f32[6,4096]{1,0:T(8,128)} async-done(((f32[6,4096]{1,0:T(8,128)}), f32[6,4096]{1,0:T(8,128)}) %all-reduce.11.cloned.1.call-update) | async-done | bytes 98320 | tf_op jit(solution)/shard_map/psum | solution.py:96
  648.1 141.3 %all-reduce.13.cloned.1.call-done = f32[6,4096]{1,0:T(8,128)} async-done(((f32[6,4096]{1,0:T(8,128)}), f32[6,4096]{1,0:T(8,128)}) %all-reduce.13.cloned.1.call-update) | async-done | bytes 98320 | tf_op jit(solution)/shard_map/psum | solution.py:96
  790.4 141.8 %all-reduce.15.cloned.1.call-done = f32[6,4096]{1,0:T(8,128)} async-done(((f32[6,4096]{1,0:T(8,128)}), f32[6,4096]{1,0:T(8,128)}) %all-reduce.15.cloned.1.call-update) | async-done | bytes 98320 | tf_op jit(solution)/shard_map/psum | solution.py:96
  941.9 59.0 %all-gather.3 = f32[128,6,256]{2,1,0:T(8,128)S(1)} all-gather(f32[1,6,256]{2,1,0:T(8,128)S(1)} %maximum_bitcast_fusion.1), channel_id=3, replica_groups=mesh['grp'=8,'dev'=16] {'grp','dev'}, dimensions={0}, use_global_device_ids=true | all-gather | bytes 792576 | tf_op jit(solution)/shard_map/all_gather | solution.py:85
  1009.3 60.2 %gather_fusion.16 = f32[16384,6]{1,0:T(8,128)} fusion(f32[6,32768]{0,1:T(8,128)} %bitcast.633, s32[16384]{0:T(1024)S(1)} %broadcast_clamp_fusion), kind=kCustom, calls=%fused_computation.16 | custom fusion | bytes 851968 | tf_op jit(solution)/shard_map/gather | solution.py:87
  1077.9 32.8 %while.84 = (s32[]{:T(128)}, f32[2,6,2048]{2,1,0:T(8,128)S(1)}, f32[3,1024]{1,0:T(4,128)S(1)}, f32[2,6,2048]{2,1,0:T(8,128)S(1)}, f32[3,1024]{1,0:T(4,128)S(1)},...) while((s32[]{:T(128)}, f32[2,6,2048]{2,1,0:T(8,128)S(1)}, ...), condition=%wide.region_52.53_spmd, body=%wide.region_45.52_spmd.sunk | while | flops 85970952 | bytes 499925 | solution.py:37
  1113.6 34.0 %while.85 = (s32[]{:T(128)}, f32[2,6,2048]{2,1,0:T(8,128)}, f32[3,1024]{1,0:T(4,128)S(1)}, f32[2,6,2048]{2,1,0:T(8,128)S(1)}, f32[3,1024]{1,0:T(4,128)S(1)}, /*i...) while((s32[]{:T(128)}, f32[2,6,2048]{2,1,0:T(8,128)}, f32[3,1024]{1,0:T(4,128)S(1)}, ...), condition=%wide.region_60.61_spmd, body=%wide.region_53.60_spmd.sunk | while | flops 85970952 | bytes 483541 | solution.py:37
  1150.1 32.8 %while.86 = (s32[]{:T(128)}, f32[2,6,2048]{2,1,0:T(8,128)S(1)}, f32[3,1024]{1,0:T(4,128)S(1)}, f32[2,6,2048]{2,1,0:T(8,128)S(1)}, f32[3,1024]{1,0:T(4,128)S(1)},...) while((s32[]{:T(128)}, f32[2,6,2048]{2,1,0:T(8,128)S(1)}, ...), condition=%wide.region_69.70_spmd, body=%wide.region_62.69_spmd.sunk | while | flops 85970952 | bytes 499925 | solution.py:37
  1183.7 32.8 %while.87 = (s32[]{:T(128)}, f32[2,6,2048]{2,1,0:T(8,128)S(1)}, f32[3,1024]{1,0:T(4,128)S(1)}, f32[2,6,2048]{2,1,0:T(8,128)S(1)}, f32[3,1024]{1,0:T(4,128)S(1)},...) while((s32[]{:T(128)}, f32[2,6,2048]{2,1,0:T(8,128)S(1)}, ...), condition=%wide.region_78.79_spmd, body=%wide.region_71.78_spmd.sunk | while | flops 85970952 | bytes 499925 | solution.py:37
  1219.8 66.7 %all-reduce.17.cloned.1.call-done = f32[6,4096]{1,0:T(8,128)} async-done(((f32[6,4096]{1,0:T(8,128)}), f32[6,4096]{1,0:T(8,128)}) %all-reduce.17.cloned.1.call-update) | async-done | bytes 98320 | tf_op jit(solution)/shard_map/psum | solution.py:96
  1287.5 141.8 %all-reduce.19.cloned.1.call-done = f32[6,4096]{1,0:T(8,128)} async-done(((f32[6,4096]{1,0:T(8,128)}), f32[6,4096]{1,0:T(8,128)}) %all-reduce.19.cloned.1.call-update) | async-done | bytes 98320 | tf_op jit(solution)/shard_map/psum | solution.py:96
  1430.3 141.2 %all-reduce.21.cloned.1.call-done = f32[6,4096]{1,0:T(8,128)} async-done(((f32[6,4096]{1,0:T(8,128)}), f32[6,4096]{1,0:T(8,128)}) %all-reduce.21.cloned.1.call-update) | async-done | bytes 98320 | tf_op jit(solution)/shard_map/psum | solution.py:96
  1572.5 142.0 %all-reduce.23.cloned.1.call-done = f32[6,4096]{1,0:T(8,128)} async-done(((f32[6,4096]{1,0:T(8,128)}), f32[6,4096]{1,0:T(8,128)}) %all-reduce.23.cloned.1.call-update) | async-done | bytes 98320 | tf_op jit(solution)/shard_map/psum | solution.py:96
  (258 shorter events, 313.2 us)
Async XLA Ops:
  7.2 501.2 %all-reduce.9.cloned.1.call-start = ((), (), s32[]{:S(2)}) async-start(), calls=%async_computation | async-start | bytes 262144 | tf_op jit(solution)/shard_map/psum | solution.py:96
  78.7 11.5 copy-start.18
  289.8 357.4 %all-reduce.11.cloned.1.call-start = ((), (), s32[]{:S(2)}) async-start(), calls=%async_computation.1 | async-start | bytes 262144 | tf_op jit(solution)/shard_map/psum | solution.py:96
  396.2 100.8 %copy-start.8 = (f32[2,6,2048]{2,1,0:T(8,128)}, f32[2,6,2048]{2,1,0:T(8,128)S(1)}, u32[]{:S(2)}) copy-start(f32[2,6,2048]{2,1,0:T(8,128)S(1)} %get-tuple-element.238) | copy-start | bytes 294916
  397.6 543.1 %copy-start.15 = (s32[1024]{0:T(1024)}, s32[1024]{0:T(1024)S(1)}, u32[]{:S(2)}) copy-start(s32[1024]{0:T(1024)S(1)} %pad_clamp_fusion) | copy-start | bytes 12292
  399.7 99.4 %copy-start.11 = (f32[3,1024]{1,0:T(4,128)S(1)}, f32[3,1024]{1,0:T(4,128)}, u32[]{:S(2)}) copy-start(f32[3,1024]{1,0:T(4,128)} %param.23) | copy-start | bytes 36868
  399.7 99.6 %copy-start.12 = (f32[3,1024]{1,0:T(4,128)S(1)}, f32[3,1024]{1,0:T(4,128)}, u32[]{:S(2)}) copy-start(f32[3,1024]{1,0:T(4,128)} %param.25) | copy-start | bytes 36868
  399.7 99.8 %copy-start.13 = (f32[3,1024]{1,0:T(4,128)S(1)}, f32[3,1024]{1,0:T(4,128)}, u32[]{:S(2)}) copy-start(f32[3,1024]{1,0:T(4,128)} %param.24) | copy-start | bytes 36868
  399.7 100.7 %copy-start.14 = (f32[3,1024]{1,0:T(4,128)S(1)}, f32[3,1024]{1,0:T(4,128)}, u32[]{:S(2)}) copy-start(f32[3,1024]{1,0:T(4,128)} %param.26) | copy-start | bytes 36868
  508.4 281.0 %all-reduce.13.cloned.1.call-start = ((), (), s32[]{:S(2)}) async-start(), calls=%async_computation.2 | async-start | bytes 262144 | tf_op jit(solution)/shard_map/psum | solution.py:96
  647.2 285.0 %all-reduce.15.cloned.1.call-start = ((), (), s32[]{:S(2)}) async-start(), calls=%async_computation.3 | async-start | bytes 262144 | tf_op jit(solution)/shard_map/psum | solution.py:96
  789.4 497.1 %all-reduce.17.cloned.1.call-start = ((), (), s32[]{:S(2)}) async-start(), calls=%async_computation.4 | async-start | bytes 262144 | tf_op jit(solution)/shard_map/psum | solution.py:96
  934.7 74.5 %copy-start.2 = (f32[3,1024]{0,1:T(8,128)}, f32[3,1024]{0,1:T(8,128)S(1)}, u32[]{:S(2)}) copy-start(f32[3,1024]{0,1:T(8,128)S(1)} %scatter_fusion) | copy-start | bytes 36868
  936.3 73.0 %copy-start = (f32[3,1024]{0,1:T(8,128)}, f32[3,1024]{0,1:T(8,128)S(1)}, u32[]{:S(2)}) copy-start(f32[3,1024]{0,1:T(8,128)S(1)} %scatter_fusion.3) | copy-start | bytes 36868
  1147.6 281.7 %all-reduce.19.cloned.1.call-start = ((), (), s32[]{:S(2)}) async-start(), calls=%async_computation.5 | async-start | bytes 262144 | tf_op jit(solution)/shard_map/psum | solution.py:96
  1183.6 32.9 %copy-start.1 = (f32[3,1024]{0,1:T(8,128)S(1)}, f32[3,1024]{0,1:T(8,128)}, u32[]{:S(2)}) copy-start(f32[3,1024]{0,1:T(8,128)} %copy-done) | copy-start | bytes 36868
  1183.6 32.9 %copy-start.16 = (s32[1024]{0:T(1024)S(1)}, s32[1024]{0:T(1024)}, u32[]{:S(2)}) copy-start(s32[1024]{0:T(1024)} %copy-done.15) | copy-start | bytes 12292
  1183.6 34.3 %copy-start.3 = (f32[3,1024]{0,1:T(8,128)S(1)}, f32[3,1024]{0,1:T(8,128)}, u32[]{:S(2)}) copy-start(f32[3,1024]{0,1:T(8,128)} %copy-done.2) | copy-start | bytes 36868
  1183.6 531.7 %copy-start.19 = (f32[256]{0:T(256)S(1)}, f32[256]{0:T(256)}, u32[]{:S(2)}) copy-start(f32[256]{0:T(256)} %get-tuple-element.731) | copy-start | bytes 3076
  1183.6 531.7 %copy-start.20 = (f32[256]{0:T(256)S(1)}, f32[256]{0:T(256)}, u32[]{:S(2)}) copy-start(f32[256]{0:T(256)} %get-tuple-element.732) | copy-start | bytes 3076
  1183.7 531.9 %copy-start.17 = (s32[256,1]{0,1:T(1,128)S(1)}, s32[256,1]{0,1:T(1,128)}, u32[]{:S(2)}) copy-start(s32[256,1]{0,1:T(1,128)} %get-tuple-element.729) | copy-start | bytes 3076
  1216.5 355.0 %copy-start.4 = (f32[2,6,2048]{2,1,0:T(8,128)}, f32[2,6,2048]{2,1,0:T(8,128)S(1)}, u32[]{:S(2)}) copy-start(f32[2,6,2048]{2,1,0:T(8,128)S(1)} %get-tuple-element.248) | copy-start | bytes 294916
  1286.5 285.0 %all-reduce.21.cloned.1.call-start = ((), (), s32[]{:S(2)}) async-start(), calls=%async_computation.6 | async-start | bytes 262144 | tf_op jit(solution)/shard_map/psum | solution.py:96
  1429.3 285.1 %all-reduce.23.cloned.1.call-start = ((), (), s32[]{:S(2)}) async-start(), calls=%async_computation.7 | async-start | bytes 262144 | tf_op jit(solution)/shard_map/psum | solution.py:96
  (5 other events, 7.3 us)
Sparse Core Ops, SparseCore 0:
  289.9 138.5 all-reduce.8
  508.5 138.5 all-reduce.10
  651.9 137.4 all-reduce.12
  794.7 137.4 all-reduce.14
  1147.8 138.6 all-reduce.16
  1291.8 137.4 all-reduce.18
  1434.0 137.4 all-reduce.20
  1577.0 137.4 all-reduce.22
where the time goes:
time: 1740 us; the launch traced here: 1730 us
  waiting for transfers between devices  913 us (52%)
  local copies, waits for them, and re-layouts  405 us (23%)
  other arithmetic  270 us (16%)
  blocking collectives  123 us (7%)
  between operations  19 us (1%)
    psum x8, waiting for transfers between devices, shards(): summed = lax.psum(terms, ('grp', 'dev'))  913 us
    reduce_sum x16, other arithmetic, pair_block(): jnp.sum(weight * (drift_z - along * gap_z), axis=1)  259 us
    gather x2, local copies, waits for them, and re-layouts, shards(): slot = owner * slot_cap + place - first[owner]  194 us
    all_gather x2, blocking collectives, shards(): gathered = lax.all_gather(targets[None], ('grp', 'dev'), axis=0, tiled=True)  123 us
    gather x2, local copies, waits for them, and re-layouts, shards(): compact = flat[:, slot]  120 us
  transfers between devices with their start and end apart: 8, of which 7 were waited for; matrix products, arithmetic and copies ran while one was open for 17% of the time, Pallas kernels for 0%

commit v1 on v0

--- a/solution.py
+++ b/solution.py
@@ -93,7 +93,9 @@
             if summed is not None:
                 terms, summed = lax.optimization_barrier((terms, summed))
                 parts.append(summed)
-            summed = lax.psum(terms, ("grp", "dev"))
+            summed = terms
+            for name in ("grp", "dev"):
+                summed = lax.psum(summed, name)
         parts.append(summed)
         parts.append(jnp.zeros((6, slot_cap), jnp.float32))
         totals = jnp.concatenate(parts, axis=1)

time: 1740 us -> 1800 us (1.034)
  waiting for transfers between devices: 913 us -> 961 us
    psum x8 -> x16, waiting for transfers between devices: 913 us -> 961 us  [shards(): summed = lax.psum(summed, name)]
  transfers between devices with their start and end apart: 8 -> 16, of which waited for: 7 -> 15; matrix products, arithmetic and copies ran while one was open for 17% -> 18% of each run, Pallas kernels for 0% -> 0%
where the time goes in v1:
time: 1800 us; the launch traced here: 1790 us
  waiting for transfers between devices  961 us (53%)
  local copies, waits for them, and re-layouts  408 us (23%)
  other arithmetic  274 us (15%)
  blocking collectives  125 us (7%)
  between operations  18.9 us (1%)
    psum x16, waiting for transfers between devices, shards(): summed = lax.psum(summed, name)  961 us
    reduce_sum x16, other arithmetic, pair_block(): jnp.sum(weight * (drift_z - along * gap_z), axis=1)  262 us
    gather x2, local copies, waits for them, and re-layouts, shards(): slot = owner * slot_cap + place - first[owner]  194 us
    all_gather x2, blocking collectives, shards(): gathered = lax.all_gather(targets[None], ('grp', 'dev'), axis=0, tiled=True)  125 us
    gather x2, local copies, waits for them, and re-layouts, shards(): compact = flat[:, slot]  120 us
  transfers between devices with their start and end apart: 16, of which 15 were waited for; matrix products, arithmetic and copies ran while one was open for 18% of the time, Pallas kernels for 0%

profile of v1, /device:TPU:1, one launch (start us, length us, event | category | flops | bytes accessed | tf_op | source)
XLA Modules:
  0.0 1789.4 jit_solution(12625883050075476323)
XLA Ops:
  14.8 63.9 %all-gather.2 = f32[128,6,256]{2,1,0:T(8,128)S(1)} all-gather(f32[1,6,256]{2,1,0:T(8,128)S(1)} %maximum_bitcast_fusion), channel_id=2, replica_groups=mesh['grp'=8,'dev'=16] {'grp','dev'}, dimensions={0}, use_global_device_ids=true | all-gather | bytes 792576 | tf_op jit(solution)/shard_map/all_gather | solution.py:85
  90.3 97.2 %gather_fusion.6 = s32[16384]{0:T(1024)S(1)} fusion(s32[128]{0:T(128)S(1)} %get-tuple-element.734, s32[16384]{0:T(1024)S(1)} %broadcast_clamp_fusion.3), kind=kCustom, calls=%fused_computation.6 | custom fusion | bytes 196608 | tf_op jit(solution)/shard_map/gather | solution.py:84
  187.7 60.2 %gather_fusion.7 = f32[16384,6]{1,0:T(8,128)} fusion(f32[6,32768]{0,1:T(8,128)} %bitcast.632, s32[16384]{0:T(1024)S(1)} %broadcast_clamp_fusion.1), kind=kCustom, calls=%fused_computation.7 | custom fusion | bytes 851968 | tf_op jit(solution)/shard_map/gather | solution.py:87
  256.3 32.9 %while.81 = (s32[]{:T(128)}, f32[2,6,2048]{2,1,0:T(8,128)S(1)}, f32[3,1024]{1,0:T(4,128)S(1)}, f32[2,6,2048]{2,1,0:T(8,128)S(1)}, f32[3,1024]{1,0:T(4,128)S(1)},...) while((s32[]{:T(128)}, f32[2,6,2048]{2,1,0:T(8,128)S(1)}, ...), condition=%wide.region_17.18_spmd, body=%wide.region_10.17_spmd.sunk | while | flops 85970952 | bytes 499925 | solution.py:37
  396.6 97.2 %gather_fusion.15 = s32[16384]{0:T(1024)S(1)} fusion(s32[128]{0:T(128)S(1)} %get-tuple-element.733, s32[16384]{0:T(1024)S(1)} %broadcast_clamp_fusion.2), kind=kCustom, calls=%fused_computation.15 | custom fusion | bytes 196608 | tf_op jit(solution)/shard_map/gather | solution.py:84
  496.9 76.3 %all-reduce.19.cloned.1.call-done = f32[6,4096]{1,0:T(8,128)} async-done(((f32[6,4096]{1,0:T(8,128)}), f32[6,4096]{1,0:T(8,128)}) %all-reduce.19.cloned.1.call-update) | async-done | bytes 98320 | tf_op jit(solution)/shard_map/psum | solution.py:98
  573.3 60.6 %all-reduce.21.cloned.1.call-done = f32[6,4096]{1,0:T(8,128)} async-done(((f32[6,4096]{1,0:T(8,128)}), f32[6,4096]{1,0:T(8,128)}) %all-reduce.21.cloned.1.call-update) | async-done | bytes 98320 | tf_op jit(solution)/shard_map/psum | solution.py:98
  633.9 84.8 %all-reduce.23.cloned.1.call-done = f32[6,4096]{1,0:T(8,128)} async-done(((f32[6,4096]{1,0:T(8,128)}), f32[6,4096]{1,0:T(8,128)}) %all-reduce.23.cloned.1.call-update) | async-done | bytes 98320 | tf_op jit(solution)/shard_map/psum | solution.py:98
  725.7 53.5 %all-reduce.25.cloned.1.call-done = f32[6,4096]{1,0:T(8,128)} async-done(((f32[6,4096]{1,0:T(8,128)}), f32[6,4096]{1,0:T(8,128)}) %all-reduce.25.cloned.1.call-update) | async-done | bytes 98320 | tf_op jit(solution)/shard_map/psum | solution.py:98
  780.2 83.9 %all-reduce.27.cloned.1.call-done = f32[6,4096]{1,0:T(8,128)} async-done(((f32[6,4096]{1,0:T(8,128)}), f32[6,4096]{1,0:T(8,128)}) %all-reduce.27.cloned.1.call-update) | async-done | bytes 98320 | tf_op jit(solution)/shard_map/psum | solution.py:98
  865.1 59.7 %all-reduce.29.cloned.1.call-done = f32[6,4096]{1,0:T(8,128)} async-done(((f32[6,4096]{1,0:T(8,128)}), f32[6,4096]{1,0:T(8,128)}) %all-reduce.29.cloned.1.call-update) | async-done | bytes 98320 | tf_op jit(solution)/shard_map/psum | solution.py:98
  925.7 84.0 %all-reduce.31.cloned.1.call-done = f32[6,4096]{1,0:T(8,128)} async-done(((f32[6,4096]{1,0:T(8,128)}), f32[6,4096]{1,0:T(8,128)}) %all-reduce.31.cloned.1.call-update) | async-done | bytes 98320 | tf_op jit(solution)/shard_map/psum | solution.py:98
  1019.4 60.8 %all-gather.3 = f32[128,6,256]{2,1,0:T(8,128)S(1)} all-gather(f32[1,6,256]{2,1,0:T(8,128)S(1)} %maximum_bitcast_fusion.1), channel_id=3, replica_groups=mesh['grp'=8,'dev'=16] {'grp','dev'}, dimensions={0}, use_global_device_ids=true | all-gather | bytes 792576 | tf_op jit(solution)/shard_map/all_gather | solution.py:85
  1088.5 60.2 %gather_fusion.16 = f32[16384,6]{1,0:T(8,128)} fusion(f32[6,32768]{0,1:T(8,128)} %bitcast.633, s32[16384]{0:T(1024)S(1)} %broadcast_clamp_fusion), kind=kCustom, calls=%fused_computation.16 | custom fusion | bytes 851968 | tf_op jit(solution)/shard_map/gather | solution.py:87
  1157.1 35.4 %while.85 = (s32[]{:T(128)}, f32[2,6,2048]{2,1,0:T(8,128)S(1)}, f32[3,1024]{1,0:T(4,128)S(1)}, f32[2,6,2048]{2,1,0:T(8,128)S(1)}, f32[3,1024]{1,0:T(4,128)S(1)},...) while((s32[]{:T(128)}, f32[2,6,2048]{2,1,0:T(8,128)S(1)}, ...), condition=%wide.region_64.65_spmd, body=%wide.region_57.64_spmd.sunk | while | flops 85970952 | bytes 499925 | solution.py:37
  1197.5 51.5 %all-reduce.33.cloned.1.call-done = f32[6,4096]{1,0:T(8,128)} async-done(((f32[6,4096]{1,0:T(8,128)}), f32[6,4096]{1,0:T(8,128)}) %all-reduce.33.cloned.1.call-update) | async-done | bytes 98320 | tf_op jit(solution)/shard_map/psum | solution.py:98
  1249.3 35.4 %while.84 = (s32[]{:T(128)}, f32[2,6,2048]{2,1,0:T(8,128)S(1)}, f32[3,1024]{1,0:T(4,128)S(1)}, f32[2,6,2048]{2,1,0:T(8,128)S(1)}, f32[3,1024]{1,0:T(4,128)S(1)},...) while((s32[]{:T(128)}, f32[2,6,2048]{2,1,0:T(8,128)S(1)}, ...), condition=%wide.region_56.57_spmd, body=%wide.region_49.56_spmd.sunk | while | flops 85970952 | bytes 499925 | solution.py:37
  1284.8 49.1 %all-reduce.35.cloned.1.call-done = f32[6,4096]{1,0:T(8,128)} async-done(((f32[6,4096]{1,0:T(8,128)}), f32[6,4096]{1,0:T(8,128)}) %all-reduce.35.cloned.1.call-update) | async-done | bytes 98320 | tf_op jit(solution)/shard_map/psum | solution.py:98
  1340.0 54.6 %all-reduce.37.cloned.1.call-done = f32[6,4096]{1,0:T(8,128)} async-done(((f32[6,4096]{1,0:T(8,128)}), f32[6,4096]{1,0:T(8,128)}) %all-reduce.37.cloned.1.call-update) | async-done | bytes 98320 | tf_op jit(solution)/shard_map/psum | solution.py:98
  1428.1 51.3 %all-reduce.39.cloned.1.call-done = f32[6,4096]{1,0:T(8,128)} async-done(((f32[6,4096]{1,0:T(8,128)}), f32[6,4096]{1,0:T(8,128)}) %all-reduce.39.cloned.1.call-update) | async-done | bytes 98320 | tf_op jit(solution)/shard_map/psum | solution.py:98
  1479.6 32.9 %while.87 = (s32[]{:T(128)}, f32[2,6,2048]{2,1,0:T(8,128)S(1)}, f32[3,1024]{1,0:T(4,128)S(1)}, f32[2,6,2048]{2,1,0:T(8,128)S(1)}, f32[3,1024]{1,0:T(4,128)S(1)},...) while((s32[]{:T(128)}, f32[2,6,2048]{2,1,0:T(8,128)S(1)}, ...), condition=%wide.region_84.85_spmd, body=%wide.region_77.84_spmd.sunk | while | flops 85970952 | bytes 499925 | solution.py:37
  1540.8 84.1 %all-reduce.43.cloned.1.call-done = f32[6,4096]{1,0:T(8,128)} async-done(((f32[6,4096]{1,0:T(8,128)}), f32[6,4096]{1,0:T(8,128)}) %all-reduce.43.cloned.1.call-update) | async-done | bytes 98320 | tf_op jit(solution)/shard_map/psum | solution.py:98
  1625.7 59.7 %all-reduce.45.cloned.1.call-done = f32[6,4096]{1,0:T(8,128)} async-done(((f32[6,4096]{1,0:T(8,128)}), f32[6,4096]{1,0:T(8,128)}) %all-reduce.45.cloned.1.call-update) | async-done | bytes 98320 | tf_op jit(solution)/shard_map/psum | solution.py:98
  1687.0 83.3 %all-reduce.47.cloned.1.call-done = f32[6,4096]{1,0:T(8,128)} async-done(((f32[6,4096]{1,0:T(8,128)}), f32[6,4096]{1,0:T(8,128)}) %all-reduce.47.cloned.1.call-update) | async-done | bytes 98320 | tf_op jit(solution)/shard_map/psum | solution.py:98
  (288 shorter events, 525.4 us)
Async XLA Ops:
  7.2 486.8 %all-reduce.17.cloned.1.call-start = ((), (), s32[]{:S(2)}) async-start(), calls=%async_computation | async-start | bytes 262144 | tf_op jit(solution)/shard_map/psum | solution.py:98
  289.8 283.4 %all-reduce.19.cloned.1.call-start = ((), (), s32[]{:S(2)}) async-start(), calls=%async_computation.1 | async-start | bytes 262144 | tf_op jit(solution)/shard_map/psum | solution.py:98
  396.6 322.4 %copy-start.14 = (f32[3,1024]{1,0:T(4,128)S(1)}, f32[3,1024]{1,0:T(4,128)}, u32[]{:S(2)}) copy-start(f32[3,1024]{1,0:T(4,128)} %param.23) | copy-start | bytes 36868
  396.6 322.6 %copy-start.15 = (f32[3,1024]{1,0:T(4,128)S(1)}, f32[3,1024]{1,0:T(4,128)}, u32[]{:S(2)}) copy-start(f32[3,1024]{1,0:T(4,128)} %param.25) | copy-start | bytes 36868
  396.6 322.9 %copy-start.16 = (f32[3,1024]{1,0:T(4,128)S(1)}, f32[3,1024]{1,0:T(4,128)}, u32[]{:S(2)}) copy-start(f32[3,1024]{1,0:T(4,128)} %param.24) | copy-start | bytes 36868
  396.6 323.7 %copy-start.17 = (f32[3,1024]{1,0:T(4,128)S(1)}, f32[3,1024]{1,0:T(4,128)}, u32[]{:S(2)}) copy-start(f32[3,1024]{1,0:T(4,128)} %param.26) | copy-start | bytes 36868
  494.0 139.8 %all-reduce.21.cloned.1.call-start = ((), (), s32[]{:S(2)}) async-start(), calls=%async_computation.2 | async-start | bytes 262144 | tf_op jit(solution)/shard_map/psum | solution.py:98
  573.2 145.5 %all-reduce.23.cloned.1.call-start = ((), (), s32[]{:S(2)}) async-start(), calls=%async_computation.3 | async-start | bytes 262144 | tf_op jit(solution)/shard_map/psum | solution.py:98
  633.9 145.3 %all-reduce.25.cloned.1.call-start = ((), (), s32[]{:S(2)}) async-start(), calls=%async_computation.4 | async-start | bytes 262144 | tf_op jit(solution)/shard_map/psum | solution.py:98
  718.7 145.3 %all-reduce.27.cloned.1.call-start = ((), (), s32[]{:S(2)}) async-start(), calls=%async_computation.5 | async-start | bytes 262144 | tf_op jit(solution)/shard_map/psum | solution.py:98
  719.0 300.3 %copy-start.18 = (s32[1024]{0:T(1024)}, s32[1024]{0:T(1024)S(1)}, u32[]{:S(2)}) copy-start(s32[1024]{0:T(1024)S(1)} %pad_clamp_fusion) | copy-start | bytes 12292
  779.2 145.5 %all-reduce.29.cloned.1.call-start = ((), (), s32[]{:S(2)}) async-start(), calls=%async_computation.6 | async-start | bytes 262144 | tf_op jit(solution)/shard_map/psum | solution.py:98
  864.1 145.6 %all-reduce.31.cloned.1.call-start = ((), (), s32[]{:S(2)}) async-start(), calls=%async_computation.7 | async-start | bytes 262144 | tf_op jit(solution)/shard_map/psum | solution.py:98
  924.7 324.3 %all-reduce.33.cloned.1.call-start = ((), (), s32[]{:S(2)}) async-start(), calls=%async_computation.8 | async-start | bytes 262144 | tf_op jit(solution)/shard_map/psum | solution.py:98
  1193.2 140.7 %all-reduce.35.cloned.1.call-start = ((), (), s32[]{:S(2)}) async-start(), calls=%async_computation.9 | async-start | bytes 262144 | tf_op jit(solution)/shard_map/psum | solution.py:98
  1249.1 145.5 %all-reduce.37.cloned.1.call-start = ((), (), s32[]{:S(2)}) async-start(), calls=%async_computation.10 | async-start | bytes 262144 | tf_op jit(solution)/shard_map/psum | solution.py:98
  1333.9 145.5 %all-reduce.39.cloned.1.call-start = ((), (), s32[]{:S(2)}) async-start(), calls=%async_computation.11 | async-start | bytes 262144 | tf_op jit(solution)/shard_map/psum | solution.py:98
  1394.6 145.5 %all-reduce.41.cloned.1.call-start = ((), (), s32[]{:S(2)}) async-start(), calls=%async_computation.12 | async-start | bytes 262144 | tf_op jit(solution)/shard_map/psum | solution.py:98
  1479.5 145.5 %all-reduce.43.cloned.1.call-start = ((), (), s32[]{:S(2)}) async-start(), calls=%async_computation.13 | async-start | bytes 262144 | tf_op jit(solution)/shard_map/psum | solution.py:98
  1479.6 292.9 %copy-start.22 = (f32[256]{0:T(256)S(1)}, f32[256]{0:T(256)}, u32[]{:S(2)}) copy-start(f32[256]{0:T(256)} %get-tuple-element.731) | copy-start | bytes 3076
  1479.6 292.9 %copy-start.23 = (f32[256]{0:T(256)S(1)}, f32[256]{0:T(256)}, u32[]{:S(2)}) copy-start(f32[256]{0:T(256)} %get-tuple-element.732) | copy-start | bytes 3076
  1479.6 293.9 %copy-start.20 = (s32[256,1]{0,1:T(1,128)S(1)}, s32[256,1]{0,1:T(1,128)}, u32[]{:S(2)}) copy-start(s32[256,1]{0,1:T(1,128)} %get-tuple-element.729) | copy-start | bytes 3076
  1540.1 145.3 %all-reduce.45.cloned.1.call-start = ((), (), s32[]{:S(2)}) async-start(), calls=%async_computation.14 | async-start | bytes 262144 | tf_op jit(solution)/shard_map/psum | solution.py:98
  1625.0 145.3 %all-reduce.47.cloned.1.call-start = ((), (), s32[]{:S(2)}) async-start(), calls=%async_computation.15 | async-start | bytes 262144 | tf_op jit(solution)/shard_map/psum | solution.py:98
  (16 other events, 784.0 us)
Sparse Core Ops, SparseCore 0:
  289.9 55.8 all-reduce.16
  494.1 78.9 all-reduce.18
  575.5 58.2 all-reduce.20
  637.2 81.4 all-reduce.22
  720.9 58.2 all-reduce.24
  782.6 81.4 all-reduce.26
  866.4 58.2 all-reduce.28
  928.2 81.4 all-reduce.30
  1193.3 55.6 all-reduce.32
  1252.4 81.4 all-reduce.34
  1336.2 58.2 all-reduce.36
  1397.9 81.4 all-reduce.38
  1481.7 58.2 all-reduce.40
  1543.4 81.4 all-reduce.42
  1627.1 58.2 all-reduce.44
  1688.8 81.4 all-reduce.46
